TPU v7x, 32 devices: a whole 2x2x4 slice. The times are simulated.
32 devices in a mesh: blk: 4 (over x, core), rep: 8 (over z, y).
Axes of the slice: x: 2, y: 2, z: 4, core: 2. Of those that a mesh axis runs over, the one named last changes fastest.
Arguments:
- features: bfloat16 [4096, 256], P(('blk', 'rep')), may hold values from -6 to 6
- weight_one: bfloat16 [256, 256], replicated, may hold values from -0.375 to 0.375
- weight_two: bfloat16 [256, 256], replicated, may hold values from -0.375 to 0.375
- tile_values: bfloat16 [4, 8, 24, 128, 128], P('blk', 'rep'), may hold values from -0.125 to 0.125
- tile_rows: int32 [4, 8, 24], P('blk', 'rep'), may hold values from 0 to 7, as said below
- tile_cols: int32 [4, 8, 24], P('blk', 'rep'), may hold values from 0 to 31, as said below
- tile_count: int32 [4, 8], P('blk', 'rep'), may hold values from 16 to 24, as said below
Outputs:
- aggregated: bfloat16 [4096, 256], P(('blk', 'rep'))
Inputs may be any that keep to these rules, and one draw needn't show every extreme that they name: `tile_rows`: block row within the holder's row group into which a tile adds; slots k >= tile_count are ignored. `tile_cols`: A tile held at rep index r has column block j * 8 + r for some j: its columns are nodes held by a device of rep index r. `tile_count`: one device holds exactly 24 live tiles.
All inputs are finite; a program needn't handle non-finite values.
Results may differ from a plain program's by a relative error of at most 0.035.
Values may be sent and summed in bfloat16 or wider, within the bound.
No kernel may reach another device: no remote copies, remote signals or barrier semaphores. Data moves between devices by JAX's collectives and lax.ppermute only.
A program may use at most 64 MiB of HBM per device.

v0:
```python
import jax
import jax.numpy as jnp
from jax import lax
from jax.sharding import PartitionSpec as P


def tile_products(panel_rows, tile_vals, local_block, block_size, feat_width):
    gathered = lax.all_gather(panel_rows, "blk", axis=0, tiled=True)
    source = gathered.reshape(-1, block_size, feat_width)[local_block]
    return jnp.einsum("kab,kbf->kaf", tile_vals, source, preferred_element_type=jnp.float32)


def body(features, weight_one, weight_two, tile_values, tile_rows, tile_cols, tile_count):
    tile_vals = tile_values[0, 0]
    tile_row = tile_rows[0, 0]
    tile_col = tile_cols[0, 0]
    live_count = tile_count[0, 0]
    feat_width = features.shape[1]
    block_size = tile_vals.shape[-1]
    rows_dev = features.shape[0]
    sub_blocks = rows_dev // block_size
    replicas = lax.axis_size("rep")
    group_blocks = sub_blocks * replicas
    tile_slots = tile_vals.shape[0]
    local_block = tile_col // (replicas * sub_blocks) * sub_blocks + tile_col % sub_blocks
    is_live = (lax.iota(jnp.int32, tile_slots) < live_count).astype(jnp.float32)
    hidden = features
    result = features
    for layer_id in range(2):
        weight = weight_one if layer_id == 0 else weight_two
        panel_rows = jnp.dot(hidden, weight, preferred_element_type=jnp.float32).astype(
            jnp.bfloat16
        )
        products = tile_products(panel_rows, tile_vals, local_block, block_size, feat_width)
        masked = products * is_live[:, None, None]
        partial_value = jax.ops.segment_sum(masked, tile_row, num_segments=group_blocks)
        partial_value = partial_value.astype(jnp.bfloat16).astype(jnp.float32)
        partial_value = partial_value.reshape(group_blocks * block_size, feat_width)
        group_sum = lax.psum(partial_value.astype(jnp.bfloat16), "rep").astype(jnp.float32)
        row_start = lax.axis_index("rep") * rows_dev
        summed = lax.dynamic_slice_in_dim(group_sum, row_start, rows_dev, 0)
        if layer_id == 0:
            hidden = jnp.maximum(summed, 0.0).astype(jnp.bfloat16)
        else:
            result = summed.astype(jnp.bfloat16)
    return result


def solution(mesh):
    in_specs = (
        P(("blk", "rep"), None),
        P(),
        P(),
        P("blk", "rep", None, None, None),
        P("blk", "rep", None),
        P("blk", "rep", None),
        P("blk", "rep"),
    )
    out_specs = P(("blk", "rep"), None)
    return jax.shard_map(body, mesh=mesh, in_specs=in_specs, out_specs=out_specs, check_vma=False)
```

profile of v0, /device:TPU:0, one launch (start us, length us, event | category | flops | bytes accessed | tf_op | source)
XLA Modules:
  0.0 204.6 jit_solution(6900066142206333216)
XLA Ops:
  6.5 0.0 copy-start
  6.5 0.0 all-reduce.3.cloned.1.call-start
  6.5 0.7 fusion.4
  7.3 1.1 convolution_convert_fusion.1
  8.4 7.2 %all_gather.6 = bf16[512,256]{1,0:T(8,128)(2,1)S(1)} all-gather(bf16[128,256]{1,0:T(8,128)(2,1)S(1)} %convolution_convert_fusion.1), channel_id=1, replica_groups=mesh['blk'=4,'rep'=8] {'blk'}, dimensions={0}, use_global_device_ids=true | all-gather | bytes 327680 | tf_op jit(solution)/shard_map/all_gather | solution.py:8
  16.3 0.6 gather_fusion
  16.9 0.0 copy-done
  16.9 2.4 %multiply_bitcast_fusion.1 = f32[24,128,256]{1,2,0:T(8,128)} fusion(bf16[24,128,256]{2,1,0:T(8,128)(2,1)S(1)} %gather_fusion, f32[24]{0:T(128)S(1)} %compare_convert_fusion, bf16[1,1,24,128,128]{4,3,2,1,0:T(8,128)(2,1)S(1)} %copy-done), kind=kOutput, calls=%fused_computation.5 | convolution fusion | flops 202113024 | bytes 5505120 | tf_op jit(solution)/shard_map/kab,kbf->kaf/dot_general | solution.py:10
  19.3 0.0 copy-start.2
  19.3 3.6 %copy.11 = f32[24,128,256]{2,1,0:T(8,128)} copy(f32[24,128,256]{1,2,0:T(8,128)} %multiply_bitcast_fusion.1) | data formatting | bytes 6291456 | tf_op jit(solution)/shard_map/mul | solution.py:35
  22.9 0.1 broadcast.95.clone
  23.0 0.0 copy-done.2
  23.0 0.0 copy-start.1
  23.0 6.1 %scatter_fusion = f32[8,128,256]{2,1,0:T(8,128)S(1)} fusion(f32[8,128,256]{2,1,0:T(8,128)S(1)} %broadcast.95.clone, s32[24]{0:T(128)S(1)} %bitcast.37, f32[24,128,256]{2,1,0:T(8,128)} %copy.11), kind=kCustom, calls=%fused_computation.2 | custom fusion | flops 786432 | bytes 9437280 | tf_op jit(solution)/shard_map/scatter-add | solution.py:36
  29.1 0.9 convert_element_type.43
  30.0 0.0 all-reduce.3.cloned.1.call-update
  30.0 0.0 all-reduce.5.cloned.1.call-start
  30.1 73.8 %all-reduce.3.cloned.1.call-done = bf16[1024,256]{1,0:T(8,128)(2,1)} async-done(((bf16[1024,256]{1,0:T(8,128)(2,1)}), bf16[1024,256]{1,0:T(8,128)(2,1)}) %all-reduce.3.cloned.1.call-update) | async-done | bytes 524304 | tf_op jit(solution)/shard_map/psum | solution.py:39
  103.9 0.0 copy-done.1
  103.9 1.0 convolution_convert_fusion
  104.9 5.8 %all_gather.7 = bf16[512,256]{1,0:T(8,128)(2,1)S(1)} all-gather(bf16[128,256]{1,0:T(8,128)(2,1)S(1)} %convolution_convert_fusion), channel_id=1, replica_groups=mesh['blk'=4,'rep'=8] {'blk'}, dimensions={0}, use_global_device_ids=true | all-gather | bytes 327680 | tf_op jit(solution)/shard_map/all_gather | solution.py:8
  110.7 0.6 gather_fusion.1
  111.3 2.4 %multiply_bitcast_fusion = f32[24,128,256]{1,2,0:T(8,128)} fusion(bf16[24,128,256]{2,1,0:T(8,128)(2,1)S(1)} %gather_fusion.1, f32[24]{0:T(128)S(1)} %compare_convert_fusion, bf16[1,1,24,128,128]{4,3,2,1,0:T(8,128)(2,1)S(1)} %copy-done), kind=kOutput, calls=%fused_computation.4 | convolution fusion | flops 202113024 | bytes 5505120 | tf_op jit(solution)/shard_map/kab,kbf->kaf/dot_general | solution.py:10
  113.7 3.6 %copy.13 = f32[24,128,256]{2,1,0:T(8,128)} copy(f32[24,128,256]{1,2,0:T(8,128)} %multiply_bitcast_fusion) | data formatting | bytes 6291456 | tf_op jit(solution)/shard_map/mul | solution.py:35
  117.3 0.1 broadcast.95
  117.4 6.1 %scatter_fusion.1 = f32[8,128,256]{2,1,0:T(8,128)S(1)} fusion(f32[8,128,256]{2,1,0:T(8,128)S(1)} %broadcast.95, s32[24]{0:T(128)S(1)} %bitcast.38, f32[24,128,256]{2,1,0:T(8,128)} %copy.13), kind=kCustom, calls=%fused_computation.3 | custom fusion | flops 786432 | bytes 9437280 | tf_op jit(solution)/shard_map/scatter-add | solution.py:36
  123.5 0.9 convert_element_type.48
  124.4 0.0 all-reduce.5.cloned.1.call-update
  124.4 71.9 %all-reduce.5.cloned.1.call-done = bf16[1024,256]{1,0:T(8,128)(2,1)} async-done(((bf16[1024,256]{1,0:T(8,128)(2,1)}), bf16[1024,256]{1,0:T(8,128)(2,1)}) %all-reduce.5.cloned.1.call-update) | async-done | bytes 524304 | tf_op jit(solution)/shard_map/psum | solution.py:39
  196.3 1.5 convert_convert_fusion
  (2 shorter events, 0.0 us)
Async XLA Ops:
  6.5 10.4 %copy-start = (bf16[1,1,24,128,128]{4,3,2,1,0:T(8,128)(2,1)S(1)}, bf16[1,1,24,128,128]{4,3,2,1,0:T(8,128)(2,1)}, u32[]{:S(2)}) copy-start(bf16[1,1,24,128,128]{4,3,2,1,0:T(8,128)(2,1)} %param.10) | copy-start | bytes 2359300
  6.5 97.4 %all-reduce.3.cloned.1.call-start = ((), (), s32[]{:S(2)}) async-start(), calls=%async_computation | async-start | bytes 1048576 | tf_op jit(solution)/shard_map/psum | solution.py:39
  19.3 3.7 %copy-start.2 = (s32[1,1,24]{2,1,0:T(1,128)S(1)}, s32[1,1,24]{2,1,0:T(1,128)}, u32[]{:S(2)}) copy-start(s32[1,1,24]{2,1,0:T(1,128)} %param.11) | copy-start | bytes 292
  23.0 80.9 %copy-start.1 = (bf16[256,256]{1,0:T(8,128)(2,1)S(1)}, bf16[256,256]{1,0:T(8,128)(2,1)}, u32[]{:S(2)}) copy-start(bf16[256,256]{1,0:T(8,128)(2,1)} %param.9) | copy-start | bytes 393220
  30.0 166.2 %all-reduce.5.cloned.1.call-start = ((), (), s32[]{:S(2)}) async-start(), calls=%async_computation.1 | async-start | bytes 1048576 | tf_op jit(solution)/shard_map/psum | solution.py:39
Sparse Core Ops, SparseCore 0:
  30.1 73.7 all-reduce.2
  124.5 71.6 all-reduce.4
where the time goes:
time: 205 us
  waiting for transfers between devices  146 us (71%)
  other arithmetic  16.1 us (8%)
  between operations  14.2 us (7%)
  blocking collectives  13 us (6%)
  local copies, waits for them, and re-layouts  8.65 us (4%)
  matrix products  6.9 us (3%)
    psum x2, waiting for transfers between devices, body(): lax.psum(partial_value.astype(jnp.bfloat16), 'rep').astype(jnp.float32)  146 us
    all_gather x2, blocking collectives, tile_products(): gathered = lax.all_gather(panel_rows, 'blk', axis=0, tiled=True)  13 us
    scatter-add x2, other arithmetic, body(): jax.ops.segment_sum(masked, tile_row, num_segments=group_blocks)  12.2 us
    mul x2, local copies, waits for them, and re-layouts, body(): masked = products * is_live[:, None, None]  7.18 us
    dot_general x2, matrix products, tile_products(): jnp.einsum('kab,kbf->kaf', tile_vals, source, preferred_element_type=jnp....  4.8 us
  transfers between devices with their start and end apart: 2, of which 2 were waited for; matrix products, arithmetic and copies ran while one was open for 0% of the time, Pallas kernels for 0%

commit v1 on v0

--- a/solution.py
+++ b/solution.py
@@ -5,7 +5,14 @@
 
 
 def tile_products(panel_rows, tile_vals, local_block, block_size, feat_width):
-    gathered = lax.all_gather(panel_rows, "blk", axis=0, tiled=True)
+    n_dev = lax.axis_size("blk")
+    right = [(i, (i + 1) % n_dev) for i in range(n_dev)]
+    parts = [panel_rows]
+    for far in range(1, n_dev):
+        parts = [lax.ppermute(parts[0], "blk", right), *parts]
+    whole = jnp.concatenate(parts, axis=0)
+    turn = (lax.axis_index("blk") + 1) * parts[-1].shape[0]
+    gathered = jnp.roll(whole, turn, axis=0)
     source = gathered.reshape(-1, block_size, feat_width)[local_block]
     return jnp.einsum("kab,kbf->kaf", tile_vals, source, preferred_element_type=jnp.float32)
 

time: 205 us -> 219 us (1.068)
  waiting for transfers between devices: 146 us -> 167 us
  blocking collectives: 13 us -> 0 us
  other arithmetic: 16.1 us -> 20.7 us
    ppermute x0 -> x6, waiting for transfers between devices: none -> 20.8 us  [tile_products(): parts = [lax.ppermute(parts[0], 'blk', right), *parts]]
    all_gather x2 -> x0, blocking collectives: 13 us -> none  [tile_products(): gathered = lax.all_gather(panel_rows, 'blk', axis=0, tiled=True)]
    concatenate x0 -> x2, other arithmetic: none -> 4.64 us  [tile_products(): gathered = jnp.roll(whole, turn, axis=0)]
  transfers between devices with their start and end apart: 2 -> 8, of which waited for: 2 -> 8; matrix products, arithmetic and copies ran while one was open for 0% -> 0% of each run, Pallas kernels for 0% -> 0%
where the time goes in v1:
time: 219 us; the launch traced here: 218 us
  waiting for transfers between devices  167 us (76%)
  other arithmetic  20.7 us (9%)
  between operations  14.2 us (6%)
  local copies, waits for them, and re-layouts  8.57 us (4%)
  matrix products  6.92 us (3%)
    psum x2, waiting for transfers between devices, body(): lax.psum(partial_value.astype(jnp.bfloat16), 'rep').astype(jnp.float32)  146 us
    ppermute x6, waiting for transfers between devices, tile_products(): parts = [lax.ppermute(parts[0], 'blk', right), *parts]  20.8 us
    scatter-add x2, other arithmetic, body(): jax.ops.segment_sum(masked, tile_row, num_segments=group_blocks)  12.2 us
    mul x2, local copies, waits for them, and re-layouts, body(): masked = products * is_live[:, None, None]  7.1 us
    dot_general x2, matrix products, tile_products(): jnp.einsum('kab,kbf->kaf', tile_vals, source, preferred_element_type=jnp....  4.76 us
    concatenate x2, other arithmetic, tile_products(): gathered = jnp.roll(whole, turn, axis=0)  4.64 us
  transfers between devices with their start and end apart: 8, of which 8 were waited for; matrix products, arithmetic and copies ran while one was open for 0% of the time, Pallas kernels for 0%

profile of v1, /device:TPU:0, one launch (start us, length us, event | category | flops | bytes accessed | tf_op | source)
XLA Modules:
  0.0 218.3 jit_solution(18236405285620745412)
XLA Ops:
  6.5 0.0 copy-start
  6.5 0.0 all-reduce.3.cloned.1.call-start
  6.5 1.2 convolution_convert_fusion.1
  7.7 0.5 collective-permute-start
  8.2 0.7 fusion.19
  9.5 2.6 %collective-permute-done = bf16[128,256]{1,0:T(8,128)(2,1)S(1)} collective-permute-done((bf16[128,256]{1,0:T(8,128)(2,1)S(1)}, bf16[128,256]{1,0:T(8,128)(2,1)S(1)}, u32[]{:S(2)}, u32[]{:S(2)}) %collective-permute-start) | collective-permute-done | bytes 65568 | tf_op jit(solution)/shard_map/ppermute | solution.py:12
  12.1 0.1 collective-permute-start.1
  12.2 3.6 %collective-permute-done.1 = bf16[128,256]{1,0:T(8,128)(2,1)S(1)} collective-permute-done((bf16[128,256]{1,0:T(8,128)(2,1)S(1)}, bf16[128,256]{1,0:T(8,128)(2,1)S(1)}, u32[]{:S(2)}, u32[]{:S(2)}) %collective-permute-start.1) | collective-permute-done | bytes 65568 | tf_op jit(solution)/shard_map/ppermute | solution.py:12
  15.8 0.1 collective-permute-start.2
  15.8 3.6 %collective-permute-done.2 = bf16[128,256]{1,0:T(8,128)(2,1)S(1)} collective-permute-done((bf16[128,256]{1,0:T(8,128)(2,1)S(1)}, bf16[128,256]{1,0:T(8,128)(2,1)S(1)}, u32[]{:S(2)}, u32[]{:S(2)}) %collective-permute-start.2) | collective-permute-done | bytes 65568 | tf_op jit(solution)/shard_map/ppermute | solution.py:12
  19.5 2.3 %fusion.12 = bf16[512,256]{1,0:T(8,128)(2,1)S(1)} fusion(s32[]{:T(128)S(6)} %select_n.48, bf16[128,256]{1,0:T(8,128)(2,1)S(1)} %collective-permute-done.2, bf16[128,256]{1,0:T(8,128)(2,1)S(1)} %collective-permute-done.1, bf16[128,256]{1,0:T(8,128)(2,1)S(1)} %collective-permute-done, bf16[128,256]{1,0:T(8,128)(2,1)S(1)} %convolution_convert_fusion.1), kind=kLoop, calls=%fused_computation.36 | loop fusion | flops 2097152 | bytes 524292 | tf_op jit(solution)/shard_map/jit(_roll_dynamic)/concatenate | solution.py:15
  21.8 0.6 gather_fusion
  22.5 0.0 copy-done
  22.5 2.4 %multiply_bitcast_fusion.1 = f32[24,128,256]{1,2,0:T(8,128)} fusion(bf16[24,128,256]{2,1,0:T(8,128)(2,1)S(1)} %gather_fusion, f32[24]{0:T(128)S(1)} %compare_convert_fusion, bf16[1,1,24,128,128]{4,3,2,1,0:T(8,128)(2,1)S(1)} %copy-done), kind=kOutput, calls=%fused_computation.5 | convolution fusion | flops 202113024 | bytes 5505120 | tf_op jit(solution)/shard_map/kab,kbf->kaf/dot_general | solution.py:17
  24.9 0.0 copy-start.2
  24.9 3.6 %copy.11 = f32[24,128,256]{2,1,0:T(8,128)} copy(f32[24,128,256]{1,2,0:T(8,128)} %multiply_bitcast_fusion.1) | data formatting | bytes 6291456 | tf_op jit(solution)/shard_map/mul | solution.py:42
  28.4 0.1 broadcast.96.clone
  28.5 0.0 copy-done.2
  28.5 0.0 copy-start.1
  28.5 6.1 %scatter_fusion = f32[8,128,256]{2,1,0:T(8,128)S(1)} fusion(f32[8,128,256]{2,1,0:T(8,128)S(1)} %broadcast.96.clone, s32[24]{0:T(128)S(1)} %bitcast.37, f32[24,128,256]{2,1,0:T(8,128)} %copy.11), kind=kCustom, calls=%fused_computation.2 | custom fusion | flops 786432 | bytes 9437280 | tf_op jit(solution)/shard_map/scatter-add | solution.py:43
  34.6 0.8 convert_element_type.43
  35.5 0.0 all-reduce.3.cloned.1.call-update
  35.5 0.0 all-reduce.5.cloned.1.call-start
  35.5 74.6 %all-reduce.3.cloned.1.call-done = bf16[1024,256]{1,0:T(8,128)(2,1)} async-done(((bf16[1024,256]{1,0:T(8,128)(2,1)}), bf16[1024,256]{1,0:T(8,128)(2,1)}) %all-reduce.3.cloned.1.call-update) | async-done | bytes 524304 | tf_op jit(solution)/shard_map/psum | solution.py:46
  110.1 0.0 copy-done.1
  110.1 1.0 convolution_convert_fusion
  111.1 0.1 collective-permute-start.3
  111.2 3.7 %collective-permute-done.3 = bf16[128,256]{1,0:T(8,128)(2,1)S(1)} collective-permute-done((bf16[128,256]{1,0:T(8,128)(2,1)S(1)}, bf16[128,256]{1,0:T(8,128)(2,1)S(1)}, u32[]{:S(2)}, u32[]{:S(2)}) %collective-permute-start.3) | collective-permute-done | bytes 65568 | tf_op jit(solution)/shard_map/ppermute | solution.py:12
  114.9 0.0 collective-permute-start.4
  114.9 3.7 %collective-permute-done.4 = bf16[128,256]{1,0:T(8,128)(2,1)S(1)} collective-permute-done((bf16[128,256]{1,0:T(8,128)(2,1)S(1)}, bf16[128,256]{1,0:T(8,128)(2,1)S(1)}, u32[]{:S(2)}, u32[]{:S(2)}) %collective-permute-start.4) | collective-permute-done | bytes 65568 | tf_op jit(solution)/shard_map/ppermute | solution.py:12
  118.5 0.0 collective-permute-start.5
  118.6 3.7 %collective-permute-done.5 = bf16[128,256]{1,0:T(8,128)(2,1)S(1)} collective-permute-done((bf16[128,256]{1,0:T(8,128)(2,1)S(1)}, bf16[128,256]{1,0:T(8,128)(2,1)S(1)}, u32[]{:S(2)}, u32[]{:S(2)}) %collective-permute-start.5) | collective-permute-done | bytes 65568 | tf_op jit(solution)/shard_map/ppermute | solution.py:12
  122.2 2.3 %fusion.5 = bf16[512,256]{1,0:T(8,128)(2,1)S(1)} fusion(s32[]{:T(128)S(6)} %select_n.48, bf16[128,256]{1,0:T(8,128)(2,1)S(1)} %collective-permute-done.5, bf16[128,256]{1,0:T(8,128)(2,1)S(1)} %collective-permute-done.4, bf16[128,256]{1,0:T(8,128)(2,1)S(1)} %collective-permute-done.3, bf16[128,256]{1,0:T(8,128)(2,1)S(1)} %convolution_convert_fusion), kind=kLoop, calls=%fused_computation.29 | loop fusion | flops 2097152 | bytes 524292 | tf_op jit(solution)/shard_map/jit(_roll_dynamic)/concatenate | solution.py:15
  124.6 0.6 gather_fusion.1
  125.2 2.4 %multiply_bitcast_fusion = f32[24,128,256]{1,2,0:T(8,128)} fusion(bf16[24,128,256]{2,1,0:T(8,128)(2,1)S(1)} %gather_fusion.1, f32[24]{0:T(128)S(1)} %compare_convert_fusion, bf16[1,1,24,128,128]{4,3,2,1,0:T(8,128)(2,1)S(1)} %copy-done), kind=kOutput, calls=%fused_computation.4 | convolution fusion | flops 202113024 | bytes 5505120 | tf_op jit(solution)/shard_map/kab,kbf->kaf/dot_general | solution.py:17
  127.6 3.5 %copy.13 = f32[24,128,256]{2,1,0:T(8,128)} copy(f32[24,128,256]{1,2,0:T(8,128)} %multiply_bitcast_fusion) | data formatting | bytes 6291456 | tf_op jit(solution)/shard_map/mul | solution.py:42
  131.1 0.1 broadcast.96
  131.2 6.1 %scatter_fusion.1 = f32[8,128,256]{2,1,0:T(8,128)S(1)} fusion(f32[8,128,256]{2,1,0:T(8,128)S(1)} %broadcast.96, s32[24]{0:T(128)S(1)} %bitcast.38, f32[24,128,256]{2,1,0:T(8,128)} %copy.13), kind=kCustom, calls=%fused_computation.3 | custom fusion | flops 786432 | bytes 9437280 | tf_op jit(solution)/shard_map/scatter-add | solution.py:43
  137.3 0.8 convert_element_type.48
  138.2 0.0 all-reduce.5.cloned.1.call-update
  138.2 71.8 %all-reduce.5.cloned.1.call-done = bf16[1024,256]{1,0:T(8,128)(2,1)} async-done(((bf16[1024,256]{1,0:T(8,128)(2,1)}), bf16[1024,256]{1,0:T(8,128)(2,1)}) %all-reduce.5.cloned.1.call-update) | async-done | bytes 524304 | tf_op jit(solution)/shard_map/psum | solution.py:46
  210.0 1.5 convert_convert_fusion
  (2 shorter events, 0.0 us)
Async XLA Ops:
  6.5 15.9 %copy-start = (bf16[1,1,24,128,128]{4,3,2,1,0:T(8,128)(2,1)S(1)}, bf16[1,1,24,128,128]{4,3,2,1,0:T(8,128)(2,1)}, u32[]{:S(2)}) copy-start(bf16[1,1,24,128,128]{4,3,2,1,0:T(8,128)(2,1)} %param.12) | copy-start | bytes 2359300
  6.5 103.6 %all-reduce.3.cloned.1.call-start = ((), (), s32[]{:S(2)}) async-start(), calls=%async_computation | async-start | bytes 1048576 | tf_op jit(solution)/shard_map/psum | solution.py:46
  7.7 4.4 %collective-permute-start = (bf16[128,256]{1,0:T(8,128)(2,1)S(1)}, bf16[128,256]{1,0:T(8,128)(2,1)S(1)}, u32[]{:S(2)}, u32[]{:S(2)}) collective-permute-start(bf16[128,256]{1,0:T(8,128)(2,1)S(1)} %convolution_convert_fusion.1), channel_id=1, source_target_pairs={{0,8},{8,16},{16,24},{24,0},{1,9},{9,17},{17,25},{25,1},{2,10},{10... | collective-permute-start | bytes 196616 | tf_op jit(solution)/shard_map/ppermute | solution.py:12
  12.1 3.7 %collective-permute-start.1 = (bf16[128,256]{1,0:T(8,128)(2,1)S(1)}, bf16[128,256]{1,0:T(8,128)(2,1)S(1)}, u32[]{:S(2)}, u32[]{:S(2)}) collective-permute-start(bf16[128,256]{1,0:T(8,128)(2,1)S(1)} %collective-permute-done), channel_id=1, source_target_pairs={{0,8},{8,16},{16,24},{24,0},{1,9},{9,17},{17,25},{25,1},{2,10},{10... | collective-permute-start | bytes 196616 | tf_op jit(solution)/shard_map/ppermute | solution.py:12
  15.8 3.7 %collective-permute-start.2 = (bf16[128,256]{1,0:T(8,128)(2,1)S(1)}, bf16[128,256]{1,0:T(8,128)(2,1)S(1)}, u32[]{:S(2)}, u32[]{:S(2)}) collective-permute-start(bf16[128,256]{1,0:T(8,128)(2,1)S(1)} %collective-permute-done.1), channel_id=1, source_target_pairs={{0,8},{8,16},{16,24},{24,0},{1,9},{9,17},{17,25},{25,1},{2,10},{10... | collective-permute-start | bytes 196616 | tf_op jit(solution)/shard_map/ppermute | solution.py:12
  24.9 3.6 %copy-start.2 = (s32[1,1,24]{2,1,0:T(1,128)S(1)}, s32[1,1,24]{2,1,0:T(1,128)}, u32[]{:S(2)}) copy-start(s32[1,1,24]{2,1,0:T(1,128)} %param.13) | copy-start | bytes 292
  28.5 81.6 %copy-start.1 = (bf16[256,256]{1,0:T(8,128)(2,1)S(1)}, bf16[256,256]{1,0:T(8,128)(2,1)}, u32[]{:S(2)}) copy-start(bf16[256,256]{1,0:T(8,128)(2,1)} %param.11) | copy-start | bytes 393220
  35.5 174.5 %all-reduce.5.cloned.1.call-start = ((), (), s32[]{:S(2)}) async-start(), calls=%async_computation.1 | async-start | bytes 1048576 | tf_op jit(solution)/shard_map/psum | solution.py:46
  111.1 3.7 %collective-permute-start.3 = (bf16[128,256]{1,0:T(8,128)(2,1)S(1)}, bf16[128,256]{1,0:T(8,128)(2,1)S(1)}, u32[]{:S(2)}, u32[]{:S(2)}) collective-permute-start(bf16[128,256]{1,0:T(8,128)(2,1)S(1)} %convolution_convert_fusion), channel_id=1, source_target_pairs={{0,8},{8,16},{16,24},{24,0},{1,9},{9,17},{17,25},{25,1},{2,10},{10... | collective-permute-start | bytes 196616 | tf_op jit(solution)/shard_map/ppermute | solution.py:12
  114.9 3.7 %collective-permute-start.4 = (bf16[128,256]{1,0:T(8,128)(2,1)S(1)}, bf16[128,256]{1,0:T(8,128)(2,1)S(1)}, u32[]{:S(2)}, u32[]{:S(2)}) collective-permute-start(bf16[128,256]{1,0:T(8,128)(2,1)S(1)} %collective-permute-done.3), channel_id=1, source_target_pairs={{0,8},{8,16},{16,24},{24,0},{1,9},{9,17},{17,25},{25,1},{2,10},{10... | collective-permute-start | bytes 196616 | tf_op jit(solution)/shard_map/ppermute | solution.py:12
  118.5 3.7 %collective-permute-start.5 = (bf16[128,256]{1,0:T(8,128)(2,1)S(1)}, bf16[128,256]{1,0:T(8,128)(2,1)S(1)}, u32[]{:S(2)}, u32[]{:S(2)}) collective-permute-start(bf16[128,256]{1,0:T(8,128)(2,1)S(1)} %collective-permute-done.4), channel_id=1, source_target_pairs={{0,8},{8,16},{16,24},{24,0},{1,9},{9,17},{17,25},{25,1},{2,10},{10... | collective-permute-start | bytes 196616 | tf_op jit(solution)/shard_map/ppermute | solution.py:12
Sparse Core Ops, SparseCore 0:
  35.6 74.4 all-reduce.2
  138.3 71.6 all-reduce.4
